TPU v7x, 256 devices: a whole 4x4x8 slice. The times are simulated.
256 devices in a mesh: row: 16 (over z_hi, y, core), col: 4 (over z_lo), pblk: 4 (over x).
Axes of the slice: x: 4, y: 4, z: 8 (z_hi: 2, z_lo: 4; z = z_hi * 4 + z_lo), core: 2. Of those that a mesh axis runs over, the one named last changes fastest.
Arguments:
- left_feat: int32 [2048, 256], P(('row', 'col', 'pblk')), may hold values from 0 to 255
- right_feat: int32 [4, 4, 64, 256], P('col', 'pblk', 'row'), may hold values from 0 to 255
- embed: bfloat16 [1024, 256], replicated, may hold values from -12 to 12
- conv_w: bfloat16 [8, 768, 256], replicated, may hold values from -0.01953125 to 0.01953125
- head: float32 [256], replicated, may hold values from -0.078125 to 0.078125
- assign: int32 [8], replicated, may hold values from 0 to 3, as said below
- proj_delta: bfloat16 [4, 256, 128], replicated, may hold values from -0.375 to 0.375
- proj_input: bfloat16 [4, 768, 128], replicated, may hold values from -0.21875 to 0.21875
Outputs:
- kernel: float32 [2048, 1024], P('row', ('col', 'pblk'))
Inputs may be any that keep to these rules, and one draw needn't show every extreme that they name: `assign`: every one of the 4 blocks is named by exactly 2 layers.
All inputs are finite; a program needn't handle non-finite values.
Results may differ from a plain program's by a relative error of at most 0.00036.
Values may be sent and summed in bfloat16 or wider, within the bound.
No kernel may reach another device: no remote copies, remote signals or barrier semaphores. Data moves between devices by JAX's collectives and lax.ppermute only.
A program may use at most 128 MiB of HBM per device.

v0:
```python
import jax
import jax.numpy as jnp
from jax import lax
from jax.sharding import Mesh, PartitionSpec as P

SEQ = 64
NFEAT = 4
VOCAB = 256
LAYERS = 8
PR = 128
PS = 128


def shift_wide(inputs):
    blank = jnp.zeros_like(inputs[:, :1])
    earlier = jnp.concatenate([blank, inputs[:, :-1]], 1)
    later_cells = jnp.concatenate([inputs[:, 1:], blank], 1)
    return jnp.concatenate([earlier, inputs, later_cells], 2)


def panels(features, embed, conv_w, head, assign, proj_delta, proj_input):
    examples = features.shape[0]
    blocks_here = proj_delta.shape[0]
    offsets = jnp.arange(NFEAT, dtype=jnp.int32) * VOCAB
    table_rows = features.reshape(examples, SEQ, NFEAT) + offsets
    table_ids = jnp.arange(NFEAT * VOCAB, dtype=jnp.int32)
    onehot = (table_rows[:, :, 0:1] == table_ids).astype(jnp.bfloat16)
    for field in range(1, NFEAT):
        onehot = onehot + (table_rows[:, :, field : field + 1] == table_ids).astype(jnp.bfloat16)
    hidden = jnp.einsum("esv,vc->esc", onehot, embed, preferred_element_type=jnp.float32)
    wides = []
    pres = []
    for layer in range(LAYERS):
        wide_input = shift_wide(hidden.astype(jnp.bfloat16))
        pre_act = jnp.einsum(
            "esk,kc->esc", wide_input, conv_w[layer], preferred_element_type=jnp.float32
        )
        wides.append(wide_input)
        pres.append(pre_act)
        hidden = hidden + jax.nn.silu(pre_act)
    grad_h = jnp.broadcast_to(head / SEQ, hidden.shape)
    block_ids = jnp.arange(blocks_here, dtype=jnp.int32)
    panel = jnp.zeros((examples, blocks_here, PR, PS), jnp.float32)
    for layer in range(LAYERS - 1, -1, -1):
        pre_act = pres[layer]
        sigmoid_z = jax.nn.sigmoid(pre_act)
        delta_low = (grad_h * sigmoid_z * (1.0 + pre_act * (1.0 - sigmoid_z))).astype(jnp.bfloat16)
        block_pick = (assign[layer] == block_ids).astype(jnp.float32)
        rows_table = jnp.einsum("b,bcr->cr", block_pick, proj_delta.astype(jnp.float32)).astype(
            jnp.bfloat16
        )
        cols_table = jnp.einsum("b,bkt->kt", block_pick, proj_input.astype(jnp.float32)).astype(
            jnp.bfloat16
        )
        left_side = jnp.einsum(
            "esc,cr->esr", delta_low, rows_table, preferred_element_type=jnp.float32
        )
        right_side = jnp.einsum(
            "esk,kt->est", wides[layer], cols_table, preferred_element_type=jnp.float32
        )
        projected = jnp.einsum(
            "esr,est->ert", left_side, right_side, precision=lax.Precision.HIGHEST
        )
        panel = panel + block_pick[None, :, None, None] * projected[:, None]
        if layer > 0:
            back_wide = jnp.einsum(
                "esc,kc->esk", delta_low, conv_w[layer], preferred_element_type=jnp.float32
            )
            width = grad_h.shape[2]
            first_third = back_wide[:, :, :width]
            last_third = back_wide[:, :, 2 * width :]
            blank = jnp.zeros_like(first_third[:, :1])
            grad_input = back_wide[:, :, width : 2 * width]
            grad_input = grad_input + jnp.concatenate([first_third[:, 1:], blank], 1)
            grad_input = grad_input + jnp.concatenate([blank, last_third[:, :-1]], 1)
            grad_h = grad_h + grad_input
    return panel.reshape(examples, blocks_here, PR * PS).astype(jnp.bfloat16)


def on_device(left_feat, right_feat, embed, conv_w, head, assign, proj_delta, proj_input):
    group = ("zh", "core", "col")
    n_group = lax.axis_size(group)
    n_zh = lax.axis_size("zh")
    n_core = lax.axis_size("core")
    n_col = lax.axis_size("col")
    n_y = lax.axis_size("y")
    n_blk = lax.axis_size("pblk")
    left_each = left_feat.shape[0]
    right_each = right_feat.shape[2]
    right_local = right_feat.reshape(right_each, right_feat.shape[3])
    own_features = jnp.concatenate([left_feat, right_local], 0)
    panel = panels(own_features, embed, conv_w, head, assign, proj_delta, proj_input)
    own = panel.shape[0]
    width = panel.shape[1] * panel.shape[2] // n_group
    sliced = panel.reshape(own, n_group, width)
    spread = lax.all_to_all(sliced, group, split_axis=1, concat_axis=0, tiled=True)
    spread = spread.reshape(n_group, own, width)
    left_part = spread[:, :left_each].reshape(n_group * left_each, width)
    right_part = spread[:, left_each:].reshape(n_group * right_each, width)
    left_tile = lax.all_gather(left_part, "pblk", axis=0, tiled=True)
    right_tile = lax.all_gather(right_part, "y", axis=0, tiled=True)
    partial_tile = jnp.einsum(
        "lk,rk->lr", left_tile, right_tile, preferred_element_type=jnp.float32
    )
    partial_tile = partial_tile.reshape(
        n_blk, n_zh, n_core, n_col, left_each, n_y, n_zh, n_core, n_col, right_each
    )
    chunks = jnp.transpose(partial_tile, (1, 2, 8, 3, 0, 4, 6, 5, 7, 9))
    chunks = chunks.reshape(n_group, n_col * n_blk * left_each, n_zh * n_y * n_core * right_each)
    block = lax.psum_scatter(chunks, group, scatter_dimension=0, tiled=True)
    return block.reshape(block.shape[1], block.shape[2])


def solution(mesh):
    n_row = mesh.shape["row"]
    fine = Mesh(
        mesh.devices.reshape(2, 4, n_row // 8, mesh.shape["col"], mesh.shape["pblk"]),
        ("zh", "y", "core", "col", "pblk"),
    )
    rows = ("zh", "y", "core")
    placed = (
        P((*rows, "col", "pblk"), None),
        P("col", "pblk", rows, None),
        P(),
        P(),
        P(),
        P(),
        P(),
        P(),
    )
    return jax.shard_map(
        on_device, mesh=fine, in_specs=placed, out_specs=P(rows, ("col", "pblk")), check_vma=False
    )
```

profile of v0, /device:TPU:1, one launch (start us, length us, event | category | flops | bytes accessed | tf_op | source)
XLA Modules:
  0.0 414.9 jit_solution(5127504593989071444)
XLA Ops:
  6.5 1.6 fusion.261
  9.4 1.2 copy.43
  10.6 0.8 fusion.161
  11.4 1.0 fusion.165
  13.0 0.8 fusion.169
  13.8 0.7 fusion.194
  14.5 1.0 fusion.173
  15.5 0.7 fusion.195
  16.2 1.0 fusion.177
  17.8 0.9 fusion.181
  19.3 0.9 fusion.185
  20.8 0.9 fusion.189
  22.4 1.9 fusion.159
  24.2 2.0 fusion.163
  26.2 1.9 fusion.167
  28.1 2.0 fusion.171
  30.1 2.0 fusion.175
  32.1 1.2 fusion.179
  33.3 1.2 fusion.183
  34.5 1.2 fusion.187
  37.8 2.8 fusion.262
  41.3 1.4 copy-done.2
  53.6 1.4 fusion.263
  56.3 0.9 fusion.69
  57.5 1.4 fusion.264
  61.1 1.4 fusion.265
  62.6 1.6 copy.65
  65.6 1.4 fusion.266
  67.1 1.6 copy.66
  70.0 1.4 fusion.267
  71.6 1.6 copy.67
  74.7 1.4 fusion.268
  76.2 1.6 copy.68
  79.2 1.4 fusion.269
  80.7 1.6 copy.69
  83.0 1.4 fusion.270
  85.2 2.4 mul.370
  87.6 5.2 %mul.371 = f32[12,16,4096]{2,1,0:T(8,128)} reshape(f32[12,4,16384]{2,1,0:T(4,128)} %mul.370) | data formatting | bytes 6291456 | tf_op jit(solution)/shard_map/mul | solution.py:64
  92.8 3.7 mul.360
  96.5 5.2 %mul.361 = f32[12,16,4096]{2,1,0:T(8,128)} reshape(f32[12,4,16384]{2,1,0:T(4,128)} %mul.360) | data formatting | bytes 6291456 | tf_op jit(solution)/shard_map/mul | solution.py:64
  101.7 3.7 mul.350
  105.4 5.4 %mul.351 = f32[12,16,4096]{2,1,0:T(8,128)} reshape(f32[12,4,16384]{2,1,0:T(4,128)} %mul.350) | data formatting | bytes 6291456 | tf_op jit(solution)/shard_map/mul | solution.py:64
  110.8 3.6 mul.340
  114.4 5.3 %mul.341 = f32[12,16,4096]{2,1,0:T(8,128)} reshape(f32[12,4,16384]{2,1,0:T(4,128)} %mul.340) | data formatting | bytes 6291456 | tf_op jit(solution)/shard_map/mul | solution.py:64
  119.7 3.6 mul.330
  123.3 5.3 %mul.331 = f32[12,16,4096]{2,1,0:T(8,128)} reshape(f32[12,4,16384]{2,1,0:T(4,128)} %mul.330) | data formatting | bytes 6291456 | tf_op jit(solution)/shard_map/mul | solution.py:64
  128.6 3.7 mul.320
  132.2 5.2 %mul.321 = f32[12,16,4096]{2,1,0:T(8,128)} reshape(f32[12,4,16384]{2,1,0:T(4,128)} %mul.320) | data formatting | bytes 6291456 | tf_op jit(solution)/shard_map/mul | solution.py:64
  137.5 2.4 mul.310
  139.9 5.2 %mul.311 = f32[12,16,4096]{2,1,0:T(8,128)} reshape(f32[12,4,16384]{2,1,0:T(4,128)} %mul.310) | data formatting | bytes 6291456 | tf_op jit(solution)/shard_map/mul | solution.py:64
  145.2 2.4 mul.300
  147.5 5.3 %mul.301 = f32[12,16,4096]{2,1,0:T(8,128)} reshape(f32[12,4,16384]{2,1,0:T(4,128)} %mul.300) | data formatting | bytes 6291456 | tf_op jit(solution)/shard_map/mul | solution.py:64
  152.8 9.6 %add_convert_fusion = bf16[12,16,4096]{2,1,0:T(8,128)(2,1)S(1)} fusion(f32[12,16,4096]{2,1,0:T(8,128)} %mul.371, f32[12,16,4096]{2,1,0:T(8,128)} %mul.361, f32[12,16,4096]{2,1,0:T(8,128)} %mul.351, f32[12,16,4096]{2,1,0:T(8,128)} %mul.341, f32[12,16,4096]{2,1,0:T(8,128)} %mul.331, f32[12,16,4096]{2,1,0:T(8,128)} %mul.321, f32[12,16,4096]{2,1,0:T(8,128)} %mul.311, ...), kind=kLoop, calls=%fused_computation | loop fusion | flops 12582912 | bytes 26739200 | tf_op jit(solution)/shard_map/convert_element_type | solution.py:77
  162.4 0.9 copy.40
  163.3 57.9 %all_to_all.15 = bf16[12,16,4096]{2,0,1:T(8,128)(2,1)S(1)} all-to-all(bf16[12,16,4096]{2,0,1:T(8,128)(2,1)S(1)} %copy.40), channel_id=1, replica_groups=mesh['zh'=2,'y'=4,'core'=2,'col'=4,'pblk'=4] {'zh','core','col'}, dimensions={1} | all-to-all | bytes 3145728 | tf_op jit(solution)/shard_map/all_to_all | solution.py:96
  221.5 1.0 reshape.112
  222.5 1.0 slice_bitcast_fusion
  223.6 31.7 %all-gather.5.cloned.1.call-done = bf16[256,4096]{1,0:T(8,128)(2,1)} async-done(((bf16[64,4096]{1,0:T(8,128)(2,1)}), bf16[256,4096]{1,0:T(8,128)(2,1)}) %all-gather.5.cloned.1.call-update) | async-done | bytes 2097168 | tf_op jit(solution)/shard_map/all_gather | solution.py:101
  255.3 52.6 %all-gather.3.cloned.1.call-done = bf16[512,4096]{1,0:T(8,128)(2,1)} async-done(((bf16[128,4096]{1,0:T(8,128)(2,1)}), bf16[512,4096]{1,0:T(8,128)(2,1)}) %all-gather.3.cloned.1.call-update) | async-done | bytes 4194320 | tf_op jit(solution)/shard_map/all_gather | solution.py:100
  307.9 4.2 %fusion.271 = f32[512,256]{0,1:T(8,128)S(1)} fusion(bf16[512,4096]{1,0:T(8,128)(2,1)} %all-gather.3.cloned.1.call-done, bf16[256,4096]{1,0:T(8,128)(2,1)} %all-gather.5.cloned.1.call-done), kind=kOutput, calls=%fused_computation.291 | convolution fusion | flops 1073741824 | bytes 6815744 | tf_op jit(solution)/shard_map/lk,rk->lr/dot_general | solution.py:102
  312.1 11.5 %reshape.113 = f32[4,2,2,4,8,4,2,2,4,4]{4,3,2,1,0,9,8,7,6,5:T(4,128)} reshape(f32[512,256]{0,1:T(8,128)S(1)} %fusion.271) | data formatting | bytes 1048576 | tf_op jit(solution)/shard_map/reshape | solution.py:105
  323.6 9.9 %copy.42 = f32[2,2,4,4,4,8,2,4,2,4]{5,4,3,9,8,7,6,2,1,0:T(4,128)} copy(f32[2,2,4,4,4,8,2,4,2,4]{5,3,1,0,4,9,2,8,6,7:T(4,128)} %bitcast.292) | data formatting | bytes 1048576 | tf_op jit(solution)/shard_map/transpose | solution.py:108
  333.5 11.1 %reshape.114 = f32[16,128,64]{1,2,0:T(8,128)} reshape(f32[2,2,4,4,4,8,2,4,2,4]{5,4,3,9,8,7,6,2,1,0:T(4,128)} %copy.42) | data formatting | bytes 1048576 | tf_op jit(solution)/shard_map/reshape | solution.py:109
  344.6 63.3 %reduce-scatter.2.cloned.1.call-done = f32[1,128,64]{1,2,0:T(8,128)} async-done(((f32[16,128,64]{1,2,0:T(8,128)}), f32[1,128,64]{1,2,0:T(8,128)}) %reduce-scatter.2.cloned.1.call-update) | async-done | bytes 32784 | tf_op jit(solution)/shard_map/reduce_scatter | solution.py:110
  (125 shorter events, 29.1 us)
Async XLA Ops:
  6.5 31.3 %copy-start = (bf16[1024,256]{1,0:T(8,128)(2,1)S(1)}, bf16[1024,256]{1,0:T(8,128)(2,1)}, u32[]{:S(2)}) copy-start(bf16[1024,256]{1,0:T(8,128)(2,1)} %param.10) | copy-start | bytes 1572868
  6.5 15.2 %copy-start.3 = (bf16[4,768,128]{2,1,0:T(8,128)(2,1)S(1)}, bf16[4,768,128]{2,1,0:T(8,128)(2,1)}, u32[]{:S(2)}) copy-start(bf16[4,768,128]{2,1,0:T(8,128)(2,1)} %param.15) | copy-start | bytes 2359300
  6.5 248.8 %all-gather.5.cloned.1.call-start = ((), (), s32[]{:S(2)}) async-start(), calls=%async_computation.3 | async-start | bytes 2621440 | tf_op jit(solution)/shard_map/all_gather | solution.py:101
  32.1 3.6 copy-start.6
  32.1 4.8 %copy-start.4 = (s32[8,256]{1,0:T(8,128)S(1)}, s32[8,256]{1,0:T(8,128)}, u32[]{:S(2)}) copy-start(s32[8,256]{1,0:T(8,128)} %param.8) | copy-start | bytes 24580
  32.1 5.0 %copy-start.5 = (s32[1,1,4,256]{3,2,1,0:T(4,128)S(1)}, s32[1,1,4,256]{3,2,1,0:T(4,128)}, u32[]{:S(2)}) copy-start(s32[1,1,4,256]{3,2,1,0:T(4,128)} %param.9) | copy-start | bytes 12292
  37.8 3.0 copy-start.11
  40.8 1.9 copy-start.2
  42.7 1.0 copy-start.10
  44.2 1.0 copy-start.9
  45.6 1.0 copy-start.8
  47.1 1.0 copy-start.7
  222.5 85.5 %all-gather.3.cloned.1.call-start = ((), (), s32[]{:S(2)}) async-start(), calls=%async_computation.2 | async-start | bytes 5242880 | tf_op jit(solution)/shard_map/all_gather | solution.py:100
  223.6 184.3 %reduce-scatter.2.cloned.1.call-start = ((), (), s32[]{:S(2)}) async-start(), calls=%async_computation.4 | async-start | bytes 557056 | tf_op jit(solution)/shard_map/reduce_scatter | solution.py:110
  333.5 74.4 %copy-start.1 = (bf16[1024,256]{1,0:T(8,128)(2,1)S(1)}, bf16[1024,256]{1,0:T(8,128)(2,1)}, u32[]{:S(2)}) copy-start(bf16[1024,256]{1,0:T(8,128)(2,1)} %param.10) | copy-start | bytes 1572868
Sparse Core Ops, SparseCore 0:
  222.6 32.7 all-gather.4
  257.1 50.7 all-gather.2
  344.8 63.1 reduce-scatter.1
where the time goes:
time: 422 us; the launch traced here: 415 us
  waiting for transfers between devices  148 us (35%)
  local copies, waits for them, and re-layouts  124 us (29%)
  blocking collectives  57.9 us (14%)
  matrix products  53.7 us (13%)
  other arithmetic  17.5 us (4%)
  between operations  14.3 us (3%)
    mul x32, local copies, waits for them, and re-layouts, panels(): panel = panel + block_pick[None, :, None, None] * projected[:, None]  68.9 us
    reduce_scatter x1, waiting for transfers between devices, on_device(): block = lax.psum_scatter(chunks, group, scatter_dimension=0, tiled=True)  63.3 us
    all_to_all x1, blocking collectives, on_device(): lax.all_to_all(sliced, group, split_axis=1, concat_axis=0, tiled=True)  57.9 us
    all_gather x1, waiting for transfers between devices, on_device(): left_tile = lax.all_gather(left_part, 'pblk', axis=0, tiled=True)  52.6 us
    all_gather x1, waiting for transfers between devices, on_device(): right_tile = lax.all_gather(right_part, 'y', axis=0, tiled=True)  31.7 us
    unnamed x43, local copies, waits for them, and re-layouts  14.8 us
    dot_general x8, matrix products, panels(): jnp.einsum('b,bkt->kt', block_pick, proj_input.astype(jnp.float32))  13.3 us
    reshape x1, local copies, waits for them, and re-layouts, on_device(): partial_tile.reshape(n_blk, n_zh, n_core, n_col, left_each, n_y, n_zh, n_...  11.5 us
  transfers between devices with their start and end apart: 3, of which 3 were waited for; matrix products, arithmetic and copies ran while one was open for 0% of the time, Pallas kernels for 0%

commit v1 on v0

--- a/solution.py
+++ b/solution.py
@@ -9,6 +9,21 @@
 LAYERS = 8
 PR = 128
 PS = 128
+
+
+def ring_apply(x, axis, dim, make, out_dim):
+    ways, here, step = (lax.axis_size(axis), lax.axis_index(axis), x.shape[dim])
+    results = []
+    for far in range(ways):
+        arriving = (
+            lax.ppermute(x, axis, [(d, (d + 1) % ways) for d in range(ways)])
+            if far + 1 < ways
+            else x
+        )
+        results.append(make(x, (here - far) % ways * step))
+        x = arriving
+    line = jnp.concatenate(results[::-1], axis=out_dim)
+    return jnp.roll(line, (here + 1) * results[0].shape[out_dim], axis=out_dim)
 
 
 def shift_wide(inputs):
@@ -97,10 +112,15 @@
     spread = spread.reshape(n_group, own, width)
     left_part = spread[:, :left_each].reshape(n_group * left_each, width)
     right_part = spread[:, left_each:].reshape(n_group * right_each, width)
-    left_tile = lax.all_gather(left_part, "pblk", axis=0, tiled=True)
     right_tile = lax.all_gather(right_part, "y", axis=0, tiled=True)
-    partial_tile = jnp.einsum(
-        "lk,rk->lr", left_tile, right_tile, preferred_element_type=jnp.float32
+    partial_tile = ring_apply(
+        left_part,
+        "pblk",
+        0,
+        lambda shard, start: jnp.einsum(
+            "lk,rk->lr", shard, right_tile, preferred_element_type=jnp.float32
+        ),
+        0,
     )
     partial_tile = partial_tile.reshape(
         n_blk, n_zh, n_core, n_col, left_each, n_y, n_zh, n_core, n_col, right_each

time: 422 us -> 422 us (level)
  matrix products: 53.7 us -> 69.2 us
  waiting for transfers between devices: 148 us -> 136 us
  local copies, waits for them, and re-layouts: 124 us -> 116 us
    ppermute x0 -> x3, waiting for transfers between devices: none -> 72.6 us  [ring_apply(): lax.ppermute(x, axis, [(d, (d + 1) % ways) for d in range(ways)])]
    all_gather x1 -> x0, waiting for transfers between devices: 52.6 us -> none  [on_device(): left_tile = lax.all_gather(left_part, 'pblk', axis=0, tiled=True)]
    all_gather x1, waiting for transfers between devices: 31.7 us -> 0.01 us  [on_device(): right_tile = lax.all_gather(right_part, 'y', axis=0, tiled=True)]
    dot_general x8, matrix products: 3.85 us -> 9.74 us  [panels(): jnp.einsum('esk,kt->est', wides[layer], cols_table, preferred_element_typ...]
    mul x32, local copies, waits for them, and re-layouts: 68.9 us -> 63.4 us  [panels(): panel = panel + block_pick[None, :, None, None] * projected[:, None]]
    unnamed x43 -> x126, local copies, waits for them, and re-layouts: 14.8 us -> 12 us
  transfers between devices with their start and end apart: 3 -> 5, of which waited for: 3 -> 4; matrix products, arithmetic and copies ran while one was open for 0% -> 0% of each run, Pallas kernels for 0% -> 0%
where the time goes in v1:
time: 422 us; the launch traced here: 415 us
  waiting for transfers between devices  136 us (32%)
  local copies, waits for them, and re-layouts  116 us (27%)
  matrix products  69.2 us (16%)
  blocking collectives  57.9 us (14%)
  other arithmetic  19.4 us (5%)
  between operations  14.9 us (4%)
    ppermute x3, waiting for transfers between devices, ring_apply(): lax.ppermute(x, axis, [(d, (d + 1) % ways) for d in range(ways)])  72.6 us
    reduce_scatter x1, waiting for transfers between devices, on_device(): block = lax.psum_scatter(chunks, group, scatter_dimension=0, tiled=True)  63.5 us
    mul x32, local copies, waits for them, and re-layouts, panels(): panel = panel + block_pick[None, :, None, None] * projected[:, None]  63.4 us
    all_to_all x1, blocking collectives, on_device(): lax.all_to_all(sliced, group, split_axis=1, concat_axis=0, tiled=True)  57.9 us
    dot_general x8, matrix products, panels(): jnp.einsum('b,bkt->kt', block_pick, proj_input.astype(jnp.float32))  15.3 us
    unnamed x126, local copies, waits for them, and re-layouts  12 us
    dot_general x8, matrix products, panels(): jnp.einsum('esr,est->ert', left_side, right_side, precision=lax.Precision...  11.3 us
    reshape x1, local copies, waits for them, and re-layouts, on_device(): partial_tile.reshape(n_blk, n_zh, n_core, n_col, left_each, n_y, n_zh, n_...  11.3 us
  transfers between devices with their start and end apart: 5, of which 4 were waited for; matrix products, arithmetic and copies ran while one was open for 0% of the time, Pallas kernels for 0%

profile of v1, /device:TPU:1, one launch (start us, length us, event | category | flops | bytes accessed | tf_op | source)
XLA Modules:
  0.0 414.6 jit_solution(7836536822213073132)
XLA Ops:
  6.5 1.2 copy.42
  7.8 1.6 fusion.262
  9.4 1.7 copy.44
  11.1 1.5 fusion.161
  12.7 1.9 fusion.159
  14.6 1.5 fusion.165
  16.1 1.9 fusion.163
  17.9 1.5 fusion.169
  19.5 1.9 fusion.167
  21.4 1.6 fusion.173
  23.0 2.0 fusion.171
  25.0 1.5 fusion.177
  26.5 1.8 fusion.175
  28.3 1.5 fusion.181
  29.8 1.9 fusion.179
  32.7 2.0 fusion.183
  35.6 1.9 fusion.187
  37.5 1.2 fusion.191
  39.8 1.1 fusion.193
  40.9 1.2 fusion.194
  45.4 2.8 fusion.263
  66.5 1.4 fusion.271
  68.6 2.4 mul.373
  71.0 5.2 %mul.374 = f32[12,16,4096]{2,1,0:T(8,128)} reshape(f32[12,4,16384]{2,1,0:T(4,128)} %mul.373) | data formatting | bytes 6291456 | tf_op jit(solution)/shard_map/mul | solution.py:79
  76.5 1.8 fusion.114
  78.4 1.4 fusion.270
  80.5 2.5 mul.363
  83.0 5.3 %mul.364 = f32[12,16,4096]{2,1,0:T(8,128)} reshape(f32[12,4,16384]{2,1,0:T(4,128)} %mul.363) | data formatting | bytes 6291456 | tf_op jit(solution)/shard_map/mul | solution.py:79
  88.5 1.7 fusion.116
  90.2 1.4 fusion.269
  92.3 2.5 mul.353
  94.8 5.4 %mul.354 = f32[12,16,4096]{2,1,0:T(8,128)} reshape(f32[12,4,16384]{2,1,0:T(4,128)} %mul.353) | data formatting | bytes 6291456 | tf_op jit(solution)/shard_map/mul | solution.py:79
  100.6 1.7 fusion.118
  102.3 1.4 fusion.268
  104.4 2.4 mul.343
  106.8 5.3 %mul.344 = f32[12,16,4096]{2,1,0:T(8,128)} reshape(f32[12,4,16384]{2,1,0:T(4,128)} %mul.343) | data formatting | bytes 6291456 | tf_op jit(solution)/shard_map/mul | solution.py:79
  112.4 1.6 fusion.120
  114.0 1.4 fusion.267
  116.2 2.4 mul.333
  118.5 5.3 %mul.334 = f32[12,16,4096]{2,1,0:T(8,128)} reshape(f32[12,4,16384]{2,1,0:T(4,128)} %mul.333) | data formatting | bytes 6291456 | tf_op jit(solution)/shard_map/mul | solution.py:79
  124.2 1.5 fusion.122
  125.6 1.4 fusion.266
  127.8 2.4 mul.323
  130.2 5.5 %mul.324 = f32[12,16,4096]{2,1,0:T(8,128)} reshape(f32[12,4,16384]{2,1,0:T(4,128)} %mul.323) | data formatting | bytes 6291456 | tf_op jit(solution)/shard_map/mul | solution.py:79
  136.5 1.4 fusion.265
  138.6 2.5 mul.313
  141.1 5.3 %mul.314 = f32[12,16,4096]{2,1,0:T(8,128)} reshape(f32[12,4,16384]{2,1,0:T(4,128)} %mul.313) | data formatting | bytes 6291456 | tf_op jit(solution)/shard_map/mul | solution.py:79
  147.2 1.4 fusion.264
  149.3 2.4 mul.303
  151.7 5.3 %mul.304 = f32[12,16,4096]{2,1,0:T(8,128)} reshape(f32[12,4,16384]{2,1,0:T(4,128)} %mul.303) | data formatting | bytes 6291456 | tf_op jit(solution)/shard_map/mul | solution.py:79
  158.3 9.6 %add_convert_fusion = bf16[12,16,4096]{2,1,0:T(8,128)(2,1)S(1)} fusion(f32[12,16,4096]{2,1,0:T(8,128)} %mul.374, f32[12,16,4096]{2,1,0:T(8,128)} %mul.364, f32[12,16,4096]{2,1,0:T(8,128)} %mul.354, f32[12,16,4096]{2,1,0:T(8,128)} %mul.344, f32[12,16,4096]{2,1,0:T(8,128)} %mul.334, f32[12,16,4096]{2,1,0:T(8,128)} %mul.324, f32[12,16,4096]{2,1,0:T(8,128)} %mul.314, ...), kind=kLoop, calls=%fused_computation | loop fusion | flops 12582912 | bytes 26739200 | tf_op jit(solution)/shard_map/convert_element_type | solution.py:92
  168.8 57.9 %all_to_all.15 = bf16[12,16,4096]{2,0,1:T(8,128)(2,1)S(1)} all-to-all(bf16[12,16,4096]{2,0,1:T(8,128)(2,1)S(1)} %copy.39), channel_id=1, replica_groups=mesh['zh'=2,'y'=4,'core'=2,'col'=4,'pblk'=4] {'zh','core','col'}, dimensions={1} | all-to-all | bytes 3145728 | tf_op jit(solution)/shard_map/all_to_all | solution.py:111
  226.7 1.1 slice_bitcast_fusion
  227.8 1.2 collective-permute-start
  230.3 23.4 %collective-permute-done = bf16[128,4096]{1,0:T(8,128)(2,1)} collective-permute-done((bf16[128,4096]{1,0:T(8,128)(2,1)}, bf16[128,4096]{1,0:T(8,128)(2,1)}, u32[]{:S(2)}, u32[]{:S(2)}) %collective-permute-start) | collective-permute-done | bytes 1048608 | tf_op jit(solution)/shard_map/ppermute | solution.py:19
  253.9 25.0 %collective-permute-done.1 = bf16[128,4096]{1,0:T(8,128)(2,1)} collective-permute-done((bf16[128,4096]{1,0:T(8,128)(2,1)}, bf16[128,4096]{1,0:T(8,128)(2,1)}, u32[]{:S(2)}, u32[]{:S(2)}) %collective-permute-start.1) | collective-permute-done | bytes 1048608 | tf_op jit(solution)/shard_map/ppermute | solution.py:19
  278.9 24.1 %collective-permute-done.2 = bf16[128,4096]{1,0:T(8,128)(2,1)} collective-permute-done((bf16[128,4096]{1,0:T(8,128)(2,1)}, bf16[128,4096]{1,0:T(8,128)(2,1)}, u32[]{:S(2)}, u32[]{:S(2)}) %collective-permute-start.2) | collective-permute-done | bytes 1048608 | tf_op jit(solution)/shard_map/ppermute | solution.py:19
  303.1 2.9 constant_dynamic-update-slice_fusion.7
  306.0 2.1 constant_dynamic-update-slice_fusion.6
  308.1 2.1 constant_dynamic-update-slice_fusion.5
  311.4 11.3 %reshape.113 = f32[4,2,2,4,8,4,2,2,4,4]{4,3,2,1,0,9,8,7,6,5:T(4,128)} reshape(f32[512,256]{0,1:T(8,128)S(1)} %copy.40) | data formatting | bytes 1048576 | tf_op jit(solution)/shard_map/reshape | solution.py:125
  322.7 10.0 %copy.41 = f32[2,2,4,4,4,8,2,4,2,4]{5,4,3,9,8,7,6,2,1,0:T(4,128)} copy(f32[2,2,4,4,4,8,2,4,2,4]{5,3,1,0,4,9,2,8,6,7:T(4,128)} %bitcast.300) | data formatting | bytes 1048576 | tf_op jit(solution)/shard_map/transpose | solution.py:128
  332.7 11.1 %reshape.114 = f32[16,128,64]{1,2,0:T(8,128)} reshape(f32[2,2,4,4,4,8,2,4,2,4]{5,4,3,9,8,7,6,2,1,0:T(4,128)} %copy.41) | data formatting | bytes 1048576 | tf_op jit(solution)/shard_map/reshape | solution.py:129
  343.8 63.5 %reduce-scatter.2.cloned.1.call-done = f32[1,128,64]{1,2,0:T(8,128)} async-done(((f32[16,128,64]{1,2,0:T(8,128)}), f32[1,128,64]{1,2,0:T(8,128)}) %reduce-scatter.2.cloned.1.call-update) | async-done | bytes 32784 | tf_op jit(solution)/shard_map/reduce_scatter | solution.py:130
  (217 shorter events, 37.2 us)
Async XLA Ops:
  6.5 38.9 %copy-start = (bf16[1024,256]{1,0:T(8,128)(2,1)S(1)}, bf16[1024,256]{1,0:T(8,128)(2,1)}, u32[]{:S(2)}) copy-start(bf16[1024,256]{1,0:T(8,128)(2,1)} %param.10) | copy-start | bytes 1572868
  6.5 296.5 %all-gather.2.cloned.1.call-start = ((), (), s32[]{:S(2)}) async-start(), calls=%async_computation.2 | async-start | bytes 2621440 | tf_op jit(solution)/shard_map/all_gather | solution.py:115
  31.6 12.9 %copy-start.42 = (s32[1,1,4,256]{3,2,1,0:T(4,128)S(1)}, s32[1,1,4,256]{3,2,1,0:T(4,128)}, u32[]{:S(2)}) copy-start(s32[1,1,4,256]{3,2,1,0:T(4,128)} %param.9) | copy-start | bytes 12292
  31.6 13.1 %copy-start.41 = (s32[8,256]{1,0:T(8,128)S(1)}, s32[8,256]{1,0:T(8,128)}, u32[]{:S(2)}) copy-start(s32[8,256]{1,0:T(8,128)} %param.8) | copy-start | bytes 24580
  45.4 3.0 copy-start.3
  48.9 0.8 copy-start.14
  49.1 0.8 copy-start.34
  49.1 0.9 copy-start.35
  50.0 0.7 copy-start.12
  50.1 0.7 copy-start.32
  50.1 0.9 copy-start.33
  51.0 0.8 copy-start.10
  51.2 0.7 copy-start.30
  51.2 0.9 copy-start.31
  52.1 0.7 copy-start.8
  52.2 0.8 copy-start.27
  52.2 0.9 copy-start.29
  53.1 0.9 copy-start.6
  53.2 0.7 copy-start.23
  53.2 0.9 copy-start.25
  53.2 1.0 copy-start.43
  54.1 0.7 copy-start.4
  54.2 0.8 copy-start.19
  54.3 1.0 copy-start.21
  55.3 0.8 copy-start.15
  55.3 0.9 copy-start.17
  63.6 1.0 copy-start.50
  64.6 0.9 copy-start.51
  71.0 5.2 %copy-start.40 = (f32[1,256,128]{2,0,1:T(1,128)S(1)}, f32[1,256,128]{2,0,1:T(1,128)}, u32[]{:S(2)}) copy-start(f32[1,256,128]{2,0,1:T(1,128)} %fusion.165) | copy-start | bytes 393220
  83.0 5.3 %copy-start.39 = (f32[1,256,128]{2,0,1:T(1,128)S(1)}, f32[1,256,128]{2,0,1:T(1,128)}, u32[]{:S(2)}) copy-start(f32[1,256,128]{2,0,1:T(1,128)} %fusion.169) | copy-start | bytes 393220
  83.0 5.5 %copy-start.13 = (bf16[12,64,256]{2,1,0:T(8,128)(2,1)S(1)}, bf16[12,64,256]{2,1,0:T(8,128)(2,1)}, u32[]{:S(2)}) copy-start(bf16[12,64,256]{2,1,0:T(8,128)(2,1)} %copy-done.12) | copy-start | bytes 1179652
  94.8 5.5 %copy-start.38 = (f32[1,256,128]{2,0,1:T(1,128)S(1)}, f32[1,256,128]{2,0,1:T(1,128)}, u32[]{:S(2)}) copy-start(f32[1,256,128]{2,0,1:T(1,128)} %fusion.173) | copy-start | bytes 393220
  94.8 5.7 %copy-start.11 = (bf16[12,64,256]{2,1,0:T(8,128)(2,1)S(1)}, bf16[12,64,256]{2,1,0:T(8,128)(2,1)}, u32[]{:S(2)}) copy-start(bf16[12,64,256]{2,1,0:T(8,128)(2,1)} %copy-done.10) | copy-start | bytes 1179652
  106.8 5.3 %copy-start.37 = (f32[1,256,128]{2,0,1:T(1,128)S(1)}, f32[1,256,128]{2,0,1:T(1,128)}, u32[]{:S(2)}) copy-start(f32[1,256,128]{2,0,1:T(1,128)} %fusion.177) | copy-start | bytes 393220
  106.8 5.6 %copy-start.9 = (bf16[12,64,256]{2,1,0:T(8,128)(2,1)S(1)}, bf16[12,64,256]{2,1,0:T(8,128)(2,1)}, u32[]{:S(2)}) copy-start(bf16[12,64,256]{2,1,0:T(8,128)(2,1)} %copy-done.8) | copy-start | bytes 1179652
  106.8 5.6 %copy-start.28 = (bf16[12,63,256]{2,1,0:T(8,128)(2,1)S(1)}, bf16[12,63,256]{2,1,0:T(8,128)(2,1)}, u32[]{:S(2)}) copy-start(bf16[12,63,256]{2,1,0:T(8,128)(2,1)} %copy-done.27) | copy-start | bytes 1161220
  118.5 5.3 %copy-start.36 = (f32[1,256,128]{2,0,1:T(1,128)S(1)}, f32[1,256,128]{2,0,1:T(1,128)}, u32[]{:S(2)}) copy-start(f32[1,256,128]{2,0,1:T(1,128)} %fusion.181) | copy-start | bytes 393220
  118.5 5.6 %copy-start.7 = (bf16[12,64,256]{2,1,0:T(8,128)(2,1)S(1)}, bf16[12,64,256]{2,1,0:T(8,128)(2,1)}, u32[]{:S(2)}) copy-start(bf16[12,64,256]{2,1,0:T(8,128)(2,1)} %copy-done.6) | copy-start | bytes 1179652
  118.5 5.6 %copy-start.24 = (bf16[12,63,256]{2,1,0:T(8,128)(2,1)S(1)}, bf16[12,63,256]{2,1,0:T(8,128)(2,1)}, u32[]{:S(2)}) copy-start(bf16[12,63,256]{2,1,0:T(8,128)(2,1)} %copy-done.23) | copy-start | bytes 1161220
  118.5 5.6 %copy-start.26 = (bf16[12,63,256]{2,1,0:T(8,128)(2,1)S(1)}, bf16[12,63,256]{2,1,0:T(8,128)(2,1)}, u32[]{:S(2)}) copy-start(bf16[12,63,256]{2,1,0:T(8,128)(2,1)} %copy-done.25) | copy-start | bytes 1161220
  130.2 5.8 %copy-start.5 = (bf16[12,64,256]{2,1,0:T(8,128)(2,1)S(1)}, bf16[12,64,256]{2,1,0:T(8,128)(2,1)}, u32[]{:S(2)}) copy-start(bf16[12,64,256]{2,1,0:T(8,128)(2,1)} %copy-done.4) | copy-start | bytes 1179652
  130.2 5.8 %copy-start.20 = (bf16[12,63,256]{2,1,0:T(8,128)(2,1)S(1)}, bf16[12,63,256]{2,1,0:T(8,128)(2,1)}, u32[]{:S(2)}) copy-start(bf16[12,63,256]{2,1,0:T(8,128)(2,1)} %copy-done.19) | copy-start | bytes 1161220
  130.2 5.8 %copy-start.22 = (bf16[12,63,256]{2,1,0:T(8,128)(2,1)S(1)}, bf16[12,63,256]{2,1,0:T(8,128)(2,1)}, u32[]{:S(2)}) copy-start(bf16[12,63,256]{2,1,0:T(8,128)(2,1)} %copy-done.21) | copy-start | bytes 1161220
  130.2 5.8 %copy-start.49 = (f32[1,768,128]{2,0,1:T(1,128)S(1)}, f32[1,768,128]{2,0,1:T(1,128)}, u32[]{:S(2)}) copy-start(f32[1,768,128]{2,0,1:T(1,128)} %fusion.183) | copy-start | bytes 1179652
  141.1 5.6 %copy-start.16 = (bf16[12,63,256]{2,1,0:T(8,128)(2,1)S(1)}, bf16[12,63,256]{2,1,0:T(8,128)(2,1)}, u32[]{:S(2)}) copy-start(bf16[12,63,256]{2,1,0:T(8,128)(2,1)} %copy-done.15) | copy-start | bytes 1161220
  141.1 5.6 %copy-start.18 = (bf16[12,63,256]{2,1,0:T(8,128)(2,1)S(1)}, bf16[12,63,256]{2,1,0:T(8,128)(2,1)}, u32[]{:S(2)}) copy-start(bf16[12,63,256]{2,1,0:T(8,128)(2,1)} %copy-done.17) | copy-start | bytes 1161220
  141.1 5.6 %copy-start.48 = (f32[1,768,128]{2,0,1:T(1,128)S(1)}, f32[1,768,128]{2,0,1:T(1,128)}, u32[]{:S(2)}) copy-start(f32[1,768,128]{2,0,1:T(1,128)} %fusion.187) | copy-start | bytes 1179652
  151.7 5.3 %copy-start.47 = (f32[4]{0:T(128)S(1)}, f32[4]{0:T(128)}, u32[]{:S(2)}) copy-start(f32[4]{0:T(128)} %fusion.191) | copy-start | bytes 52
  151.7 5.5 %copy-start.46 = (f32[4]{0:T(128)S(1)}, f32[4]{0:T(128)}, u32[]{:S(2)}) copy-start(f32[4]{0:T(128)} %fusion.192) | copy-start | bytes 52
  151.7 5.6 %copy-start.45 = (f32[4]{0:T(128)S(1)}, f32[4]{0:T(128)}, u32[]{:S(2)}) copy-start(f32[4]{0:T(128)} %fusion.193) | copy-start | bytes 52
  151.7 5.8 %copy-start.44 = (f32[4]{0:T(128)S(1)}, f32[4]{0:T(128)}, u32[]{:S(2)}) copy-start(f32[4]{0:T(128)} %fusion.194) | copy-start | bytes 52
  227.8 25.9 %collective-permute-start = (bf16[128,4096]{1,0:T(8,128)(2,1)}, bf16[128,4096]{1,0:T(8,128)(2,1)}, u32[]{:S(2)}, u32[]{:S(2)}) collective-permute-start(bf16[128,4096]{1,0:T(8,128)(2,1)} %slice_bitcast_fusion), channel_id=1, source_target_pairs={{0,1},{1,2},{2,3},{3,0},{4,5},{5,6},{6,7},{7,4},{8,9},{9,10},{10,1... | collective-permute-start | bytes 3145736 | tf_op jit(solution)/shard_map/ppermute | solution.py:19
  230.2 177.1 %reduce-scatter.2.cloned.1.call-start = ((), (), s32[]{:S(2)}) async-start(), calls=%async_computation.3 | async-start | bytes 557056 | tf_op jit(solution)/shard_map/reduce_scatter | solution.py:130
  253.7 25.2 %collective-permute-start.1 = (bf16[128,4096]{1,0:T(8,128)(2,1)}, bf16[128,4096]{1,0:T(8,128)(2,1)}, u32[]{:S(2)}, u32[]{:S(2)}) collective-permute-start(bf16[128,4096]{1,0:T(8,128)(2,1)} %collective-permute-done), channel_id=1, source_target_pairs={{0,1},{1,2},{2,3},{3,0},{4,5},{5,6},{6,7},{7,4},{8,9},{9,10},{10,1... | collective-permute-start | bytes 3145736 | tf_op jit(solution)/shard_map/ppermute | solution.py:19
  278.9 24.1 %collective-permute-start.2 = (bf16[128,4096]{1,0:T(8,128)(2,1)}, bf16[128,4096]{1,0:T(8,128)(2,1)}, u32[]{:S(2)}, u32[]{:S(2)}) collective-permute-start(bf16[128,4096]{1,0:T(8,128)(2,1)} %collective-permute-done.1), channel_id=1, source_target_pairs={{0,1},{1,2},{2,3},{3,0},{4,5},{5,6},{6,7},{7,4},{8,9},{9,10},{10,1... | collective-permute-start | bytes 3145736 | tf_op jit(solution)/shard_map/ppermute | solution.py:19
  303.1 2.9 copy-start.2
  332.7 74.7 %copy-start.1 = (bf16[1024,256]{1,0:T(8,128)(2,1)S(1)}, bf16[1024,256]{1,0:T(8,128)(2,1)}, u32[]{:S(2)}) copy-start(bf16[1024,256]{1,0:T(8,128)(2,1)} %param.10) | copy-start | bytes 1572868
Sparse Core Ops, SparseCore 0:
  230.3 32.7 all-gather.1
  343.9 63.3 reduce-scatter.1
